TPU v7x, 32 devices: a whole 2x2x4 slice. The times are simulated.
32 devices in a mesh: grp: 2 (over x), chan: 16 (over z, y, core).
Axes of the slice: x: 2, y: 2, z: 4, core: 2. Of those that a mesh axis runs over, the one named last changes fastest.
Arguments:
- samples: bfloat16 [128, 62, 8192], P('chan', 'grp'), parts along dimension 1, may hold values from -6 to 6
- eq_gain: float32 [128, 4096], P('chan'), may hold values from 0.5 to 2
- delays: float32 [1024, 64], replicated, may hold values from -64 to 64
Outputs:
- beams: bfloat16 [2, 1024, 4096], P('grp', 'chan'), parts along dimension 0
There are 2 independent parts, one for each index of `grp`. A program takes and returns all parts, laid end to end along the dimension named above; an argument that names none is the same for every part. Nothing has to cross between parts.
All inputs are finite; a program needn't handle non-finite values.
Results may differ from a plain program's by a relative error of at most 0.0034.
Values may be sent and summed in bfloat16 or wider, within the bound.
No kernel may reach another device: no remote copies, remote signals or barrier semaphores. Data moves between devices by JAX's collectives and lax.ppermute only.
A program may use at most 448 MiB of HBM per device.

v0:
```python
import math
import jax
import jax.numpy as jnp
from jax import lax
from jax.sharding import PartitionSpec as P

DISHES = 64
POLS = 2
NB = 1024
TAPS = 16
AVG = 16
SPEC = 16


def pfb_taps(frame_len, tap_count):
    tap_total = tap_count * frame_len
    position = jnp.arange(tap_total, dtype=jnp.float32) + 0.5
    window = 0.5 - 0.5 * jnp.cos(2.0 * math.pi / tap_total * position)
    offset = (position - 0.5 * tap_total) / frame_len
    prototype = window * jnp.sin(math.pi * offset) / (math.pi * offset)
    prototype = prototype / jnp.sqrt(jnp.sum(prototype * prototype))
    return prototype.reshape(tap_count, frame_len)


def cos_sin(numer, denom):
    phase_angle = 2.0 * math.pi / denom * numer.astype(jnp.float32)
    return (jnp.cos(phase_angle), -jnp.sin(phase_angle))


def turn_tables(frame_len):
    outer_len = 2 ** ((frame_len.bit_length() - 1) // 2)
    inner_len = frame_len // outer_len
    half_len = inner_len // 2
    outer_index = jnp.arange(outer_len, dtype=jnp.int32)
    inner_index = jnp.arange(inner_len, dtype=jnp.int32)
    half_index = jnp.arange(half_len, dtype=jnp.int32)
    one_cos, one_sin = cos_sin(outer_index[:, None] * outer_index[None, :] % outer_len, outer_len)
    twist_cos, twist_sin = cos_sin(
        outer_index[:, None] * inner_index[None, :] % frame_len, frame_len
    )
    three_cos, three_sin = cos_sin(
        inner_index[:, None] * half_index[None, :] % inner_len, inner_len
    )
    table_one = jnp.stack([one_cos, one_sin])
    table_three = jnp.stack([three_cos, three_sin])
    return (outer_len, inner_len, table_one, twist_cos, twist_sin, table_three)


def body(samples, eq_gain, delays):
    inputs_here, frame_count, frame_len = samples.shape
    chan_count = frame_len // 2
    groups = lax.axis_size("chan")
    my_index = lax.axis_index("chan")
    chan_here = chan_count // groups
    beams_here = NB // groups
    time_bins = SPEC // AVG
    highest = lax.Precision.HIGHEST
    tap_table = pfb_taps(frame_len, TAPS)
    filtered = jnp.zeros((inputs_here, SPEC, frame_len), jnp.float32)
    for tap_index in range(TAPS):
        filtered = filtered + tap_table[tap_index] * samples[
            :, tap_index : tap_index + SPEC, :
        ].astype(jnp.float32)
    outer_len, inner_len, table_one, twist_cos, twist_sin, table_three = turn_tables(frame_len)
    framed = filtered.reshape(inputs_here, SPEC, outer_len, inner_len)
    section_one = jnp.einsum("rkn,isnm->irskm", table_one, framed, precision=highest)
    real_one = section_one[:, 0]
    imag_one = section_one[:, 1]
    twisted = jnp.stack(
        [real_one * twist_cos - imag_one * twist_sin, real_one * twist_sin + imag_one * twist_cos],
        axis=1,
    )
    section_three = jnp.einsum("irskm,qmj->irqsjk", twisted, table_three, precision=highest)
    spec_real = (section_three[:, 0, 0] - section_three[:, 1, 1]).reshape(
        inputs_here, SPEC, chan_count
    )
    spec_imag = (section_three[:, 0, 1] + section_three[:, 1, 0]).reshape(
        inputs_here, SPEC, chan_count
    )
    gain_row = eq_gain[:, None, :]
    voltages = jnp.stack(
        [(spec_real * gain_row).astype(jnp.bfloat16), (spec_imag * gain_row).astype(jnp.bfloat16)],
        axis=1,
    )
    row_width = chan_here * inputs_here * 2 * AVG
    outgoing = (
        voltages.reshape(inputs_here, 2, time_bins, AVG, chan_count)
        .transpose(2, 4, 0, 1, 3)
        .reshape(time_bins, groups, row_width)
    )
    channel = (my_index * chan_here + jnp.arange(chan_here, dtype=jnp.int32)).astype(jnp.float32)
    phase_turns = channel[:, None, None] * delays[None, :, :] / frame_len
    phase_angle = 2.0 * math.pi * phase_turns
    weight_scale = 1.0 / math.sqrt(DISHES)
    w_real = (jnp.cos(phase_angle) * weight_scale).astype(jnp.bfloat16)
    w_imag = (-jnp.sin(phase_angle) * weight_scale).astype(jnp.bfloat16)
    weight_stack = jnp.stack(
        [jnp.stack([w_real, -w_imag], axis=-1), jnp.stack([w_imag, w_real], axis=-1)], axis=1
    )
    block_count = math.gcd(chan_here, 8)
    block_len = chan_here // block_count
    weight_blocks = weight_stack.reshape(block_count, block_len, 2, NB, DISHES, 2)
    arrived = lax.all_to_all(outgoing, "chan", split_axis=1, concat_axis=1, tiled=True)
    item_count = arrived.shape[0]
    volt_grid = arrived.reshape(item_count, groups, chan_here, inputs_here, 2, AVG)
    volt_grid = volt_grid.transpose(2, 1, 3, 4, 0, 5).reshape(
        block_count, block_len, DISHES, POLS, 2, item_count, AVG
    )

    def one_block(block_pair):
        weight_part, volt_part = block_pair
        product = jnp.einsum(
            "cobdr,cdprqa->cobpqa", weight_part, volt_part, preferred_element_type=jnp.float32
        )
        return jnp.sum(product * product, axis=(1, 3, 5)) / AVG

    energy = lax.map(one_block, (weight_blocks, volt_grid))
    power_bins = energy.reshape(chan_here, NB, item_count).transpose(2, 1, 0).astype(jnp.bfloat16)
    sending = power_bins.reshape(item_count, groups, beams_here * chan_here)
    landed = lax.all_to_all(sending, "chan", split_axis=1, concat_axis=1, tiled=True)
    return (
        landed.reshape(time_bins, groups, beams_here, chan_here)
        .transpose(0, 2, 1, 3)
        .reshape(time_bins, beams_here, chan_count)
    )


def solution(mesh):
    in_specs = (P("chan", "grp", None), P("chan", None), P())
    out_specs = P("grp", "chan", None)
    return jax.shard_map(body, mesh=mesh, in_specs=in_specs, out_specs=out_specs, check_vma=False)
```

profile of v0, /device:TPU:0, one launch (start us, length us, event | category | flops | bytes accessed | tf_op | source)
XLA Modules:
  0.0 906.9 jit_solution(4844415604220031745)
XLA Ops:
  0.1 4.2 fusion.34
  5.4 3.6 fusion.29
  9.0 16.7 %add_bitcast_fusion = f32[8,16,64,128,1]{3,0,2,1,4:T(8,128)S(1)} fusion(bf16[8,31,8192]{2,0,1:T(8,128)(2,1)} %param.5, f32[8192]{0:T(1024)S(1)} %get-tuple-element.53, f32[8192]{0:T(1024)S(1)} %get-tuple-element.54, f32[8192]{0:T(1024)S(1)} %get-tuple-element.55, f32[8192]{0:T(1024)S(1)} %get-tuple-element.56, f32[8192]{0:T(1024)S(1)} %get-tuple-element.57, ...), kind=kLoop, calls=%fused_computation.26 | loop fusion | flops 49283072 | bytes 38273024 | tf_op jit(solution)/shard_map/reshape | solution.py:65
  25.8 7.2 fusion.18
  35.1 27.6 %fusion.12 = f32[8,2,2,16,64,64]{5,4,3,1,0,2:T(8,128)} fusion(f32[1,128,64]{1,2,0:T(8,128)S(1)} %get-tuple-element.76, f32[1,128,64]{1,2,0:T(8,128)S(1)} %get-tuple-element.77, f32[8,1,16,64,128]{4,3,1,2,0:T(8,128)S(1)} %get-tuple-element.51, f32[8,1,16,64,128]{4,3,1,2,0:T(8,128)S(1)} %get-tuple-element.50), kind=kOutput, calls=%fused_computation.18 | convolution fusion | flops 3223339008 | bytes 16842752 | tf_op jit(solution)/shard_map/irskm,qmj->irqsjk/dot_general | solution.py:73
  62.6 12.0 %slice_subtract_fusion = (f32[8,1,1,16,64,64]{5,4,3,1,0,2:T(8,128)}, f32[8,1,1,16,64,64]{5,4,3,1,0,2:T(8,128)}) fusion(f32[8,2,2,16,64,64]{5,4,3,1,0,2:T(8,128)} %fusion.12), kind=kLoop, calls=%fused_computation.21 | loop fusion | flops 1048576 | bytes 12582912 | tf_op jit(solution)/shard_map/sub | solution.py:74
  74.7 3.5 sub.38
  78.2 4.8 add.166
  85.2 27.8 %copy.27 = bf16[1,4096,8,2,16]{4,3,2,1,0:T(2,128)(2,1)} copy(bf16[1,4096,8,2,16]{1,4,3,2,0:T(8,128)(2,1)S(1)} %maximum_bitcast_fusion) | data formatting | bytes 4194304 | tf_op jit(solution)/shard_map/transpose | solution.py:88
  113.0 18.3 %reshape.393 = bf16[1,16,65536]{2,0,1:T(2,128)(2,1)} reshape(bf16[1,4096,8,2,16]{4,3,2,1,0:T(2,128)(2,1)} %copy.27) | data formatting | bytes 4194304 | tf_op jit(solution)/shard_map/reshape | solution.py:89
  131.9 13.0 %reduce.6 = bf16[16,65536]{1,0:T(8,128)(2,1)S(1)} reduce(bf16[16,1,65536]{2,1,0:T(2,128)(2,1)} %bitcast.92, bf16[]{:T(256)} %broadcast.400), dimensions={1}, to_apply=%bitcast.78.reduce_sub_computation | reduce | bytes 4194306
  147.8 7.3 all-to-all-start
  155.2 251.5 %multiply_convert_fusion = (bf16[8,32,1,1024,64,1]{3,4,5,2,1,0:T(8,128)(2,1)}, bf16[8,32,1,1024,64,1]{3,4,5,2,1,0:T(8,128)(2,1)}) fusion(f32[1024,64]{0,1:T(8,128)S(1)} %copy-done, f32[8,32]{1,0:T(8,128)S(1)} %add_convert_fusion), kind=kLoop, calls=%fused_computation.11 | loop fusion | flops 117440512 | bytes 67372032 | tf_op jit(solution)/shard_map/convert_element_type | solution.py:96
  406.7 229.4 %fusion.15 = bf16[8,32,1,1024,64,1]{3,4,5,2,1,0:T(8,128)(2,1)} fusion(f32[1024,64]{0,1:T(8,128)S(1)} %copy-done, f32[8,32]{1,0:T(8,128)S(1)} %add_convert_fusion), kind=kLoop, calls=%fused_computation.19 | loop fusion | flops 134217728 | bytes 33817600 | tf_op jit(solution)/shard_map/neg | solution.py:98
  636.1 86.9 %maximum_maximum_fusion = bf16[8,32,2,1024,64,2]{3,4,5,2,1,0:T(8,128)(2,1)} fusion(bf16[8,32,1,1024,64,1]{3,4,5,2,1,0:T(8,128)(2,1)} %get-tuple-element.69, bf16[8,32,1,1024,64,1]{3,4,5,2,1,0:T(8,128)(2,1)} %get-tuple-element.68, bf16[8,32,1,1024,64,1]{3,4,5,2,1,0:T(8,128)(2,1)} %fusion.15), kind=kLoop, calls=%fused_computation.10 | loop fusion | flops 201326592 | bytes 234881024 | tf_op jit(solution)/shard_map/stack | solution.py:97
  723.0 6.8 reshape.398
  729.8 13.2 %bitcast_reduce_fusion = bf16[16,65536]{1,0:T(8,128)(2,1)S(1)} fusion(bf16[16,1,65536]{2,1,0:T(2,128)(2,1)} %reshape.398), kind=kLoop, calls=%fused_computation.91 | loop fusion | bytes 4194304 | tf_op jit(solution)/shard_map/all_to_all | solution.py:103
  743.0 20.1 %reshape.381 = bf16[1,16,256,8,2,16]{5,4,3,2,1,0:T(2,128)(2,1)} reshape(bf16[16,65536]{1,0:T(8,128)(2,1)S(1)} %bitcast_reduce_fusion) | data formatting | bytes 4194304 | tf_op jit(solution)/shard_map/reshape | solution.py:105
  763.1 35.2 %copy.29 = bf16[256,16,8,2,1,16]{0,5,3,2,1,4:T(8,128)(2,1)S(1)} copy(bf16[256,16,8,2,1,16]{5,3,2,0,1,4:T(2,128)(2,1)} %bitcast.91) | data formatting | bytes 4194304 | tf_op jit(solution)/shard_map/transpose | solution.py:106
  798.3 6.2 reshape.382
  804.5 13.3 %copy.30 = bf16[8,32,64,2,2,1,16]{2,6,4,3,1,5,0:T(8,128)(2,1)} copy(bf16[8,32,64,2,2,1,16]{1,0,6,4,3,2,5:T(8,128)(2,1)} %reshape.382) | data formatting | bytes 4194304 | tf_op jit(solution)/shard_map/while | solution.py:117
  817.8 59.0 %while.10 = (s32[]{:T(128)}, bf16[8,32,1024,1]{2,3,1,0:T(2,128)(2,1)S(1)}, bf16[8,32,2,1024,64,2]{3,4,5,2,1,0:T(8,128)(2,1)}, bf16[8,32,64,2,2,1,16]{2,6,4,3,1,5,0:T(8,128)(2,1)}, s32[]{:T(128)}) while((s32[]{:T(128)}, bf16[8,32,1024,1]{2,3,1,0:T(2,128)(2,1)S(1)}, bf16[8,32,2,1024,64,2]{3,4,5,2,1,0:T(8,128)(2,1)}, ...), condition=%wide.region_3.4_spmd, body=%wide.region_1.3_spmd.sunk | while | flops 541097984 | bytes 17826888 | solution.py:117
  817.8 7.2 fusion.68
  825.2 7.2 fusion.68
  832.6 7.3 fusion.68
  839.9 7.3 fusion.68
  847.3 7.2 fusion.68
  854.7 7.2 fusion.68
  862.1 7.3 fusion.68
  869.5 7.3 fusion.68
  877.7 3.7 reduce.7
  881.9 20.3 %all_to_all.10 = bf16[16,2,8192]{2,1,0:T(2,128)(2,1)S(1)} all-to-all(bf16[16,2,8192]{2,1,0:T(2,128)(2,1)S(1)} %reshape.399), channel_id=1, replica_groups=mesh['grp'=2,'chan'=16] {'chan'}, dimensions={0} | all-to-all | bytes 1048576 | tf_op jit(solution)/shard_map/all_to_all | solution.py:120
  (41 shorter events, 14.7 us)
Async XLA Ops:
  78.2 4.8 copy-start.1
  144.9 10.3 %copy-start = (f32[1024,64]{0,1:T(8,128)S(1)}, f32[1024,64]{0,1:T(8,128)}, u32[]{:S(2)}) copy-start(f32[1024,64]{0,1:T(8,128)} %param.7) | copy-start | bytes 786436
  147.8 575.2 %all-to-all-start = ((bf16[16,2,32768]{2,1,0:T(2,128)(2,1)}), bf16[16,2,32768]{2,1,0:T(2,128)(2,1)S(1)}, u32[]{:S(2)}, u32[]{:S(2)}) async-start(bf16[16,2,32768]{2,1,0:T(2,128)(2,1)} %reshape.397), calls=%async_computation | async-start | bytes 4194304 | tf_op jit(solution)/shard_map/all_to_all | solution.py:103
where the time goes:
time: 916 us; the launch traced here: 907 us
  other arithmetic  626 us (68%)
  local copies, waits for them, and re-layouts  159 us (17%)
  matrix products  92.8 us (10%)
  blocking collectives  20.3 us (2%)
    convert_element_type x1, other arithmetic, body(): w_imag = (-jnp.sin(phase_angle) * weight_scale).astype(jnp.bfloat16)  251 us
    neg x1, other arithmetic, body(): -w_imag  229 us
    another operation x1, other arithmetic, body(): jnp.stack([jnp.stack([w_real, -w_imag], axis=-1), jnp.stack([w_imag, w_re...  86.9 us
    dot_general x8, matrix products, one_block(): jnp.einsum('cobdr,cdprqa->cobpqa', weight_part, volt_part, preferred_elem...  58 us
    transpose x1, local copies, waits for them, and re-layouts, body(): volt_grid.transpose(2, 1, 3, 4, 0, 5)  35.2 us
    transpose x1, local copies, waits for them, and re-layouts, body(): outgoing = voltages.reshape(inputs_here, 2, time_bins, AVG, chan_count).t...  27.8 us
    dot_general x1, matrix products, body(): jnp.einsum('irskm,qmj->irqsjk', twisted, table_three, precision=highest)  27.6 us
    all_to_all x1, blocking collectives, body(): lax.all_to_all(sending, 'chan', split_axis=1, concat_axis=1, tiled=True)  20.3 us
  transfers between devices with their start and end apart: 1, of which 0 were waited for; matrix products, arithmetic and copies ran while one was open for 63% of the time, Pallas kernels for 0%

commit v1 on v0

--- a/solution.py
+++ b/solution.py
@@ -100,7 +100,19 @@
     block_count = math.gcd(chan_here, 8)
     block_len = chan_here // block_count
     weight_blocks = weight_stack.reshape(block_count, block_len, 2, NB, DISHES, 2)
-    arrived = lax.all_to_all(outgoing, "chan", split_axis=1, concat_axis=1, tiled=True)
+    ways, here = (lax.axis_size("chan"), lax.axis_index("chan"))
+    width = outgoing.shape[1] // ways
+    dims = list(outgoing.shape)
+    dims[1] = width
+    height = dims[1]
+    dims[1] = height * ways
+    full = jnp.zeros(dims, outgoing.dtype)
+    for mask in range(ways):
+        part = lax.dynamic_slice_in_dim(outgoing, (here ^ mask) * width, width, axis=1)
+        if mask:
+            part = lax.ppermute(part, "chan", [(d, d ^ mask) for d in range(ways)])
+        full = lax.dynamic_update_slice_in_dim(full, part, (here ^ mask) * height, axis=1)
+    arrived = full
     item_count = arrived.shape[0]
     volt_grid = arrived.reshape(item_count, groups, chan_here, inputs_here, 2, AVG)
     volt_grid = volt_grid.transpose(2, 1, 3, 4, 0, 5).reshape(

time: 916 us -> 1020 us (1.11)
  local copies, waits for them, and re-layouts: 159 us -> 253 us
  starting transfers between devices: 7.35 us -> 22.4 us
  other arithmetic: 626 us -> 612 us
    dynamic_update_slice x0 -> x16, local copies, waits for them, and re-layouts: none -> 87.4 us  [body(): lax.dynamic_update_slice_in_dim(full, part, (here ^ mask) * height, axis=1)]
    ppermute x0 -> x15, starting transfers between devices: none -> 22.4 us  [body(): part = lax.ppermute(part, 'chan', [(d, d ^ mask) for d in range(ways)])]
    reshape x1, local copies, waits for them, and re-layouts: 18.3 us -> 40.3 us  [body(): outgoing = voltages.reshape(inputs_here, 2, time_bins, AVG, chan_count).t...]
    all_to_all x1 -> x0, local copies, waits for them, and re-layouts: 13.2 us -> none  [body(): lax.all_to_all(outgoing, 'chan', split_axis=1, concat_axis=1, tiled=True)]
    unnamed x2 -> x1, other arithmetic: 16.7 us -> 3.79 us
  transfers between devices with their start and end apart: 1 -> 15, of which waited for: 0 -> 0; matrix products, arithmetic and copies ran while one was open for 63% -> 65% of each run, Pallas kernels for 0% -> 0%
where the time goes in v1:
time: 1020 us; the launch traced here: 1000 us
  other arithmetic  612 us (60%)
  local copies, waits for them, and re-layouts  253 us (25%)
  matrix products  93.1 us (9%)
  starting transfers between devices  22.4 us (2%)
  blocking collectives  19.4 us (2%)
    convert_element_type x1, other arithmetic, body(): w_imag = (-jnp.sin(phase_angle) * weight_scale).astype(jnp.bfloat16)  251 us
    neg x1, other arithmetic, body(): -w_imag  229 us
    dynamic_update_slice x16, local copies, waits for them, and re-layouts, body(): lax.dynamic_update_slice_in_dim(full, part, (here ^ mask) * height, axis=1)  87.4 us
    another operation x1, other arithmetic, body(): jnp.stack([jnp.stack([w_real, -w_imag], axis=-1), jnp.stack([w_imag, w_re...  86.9 us
    dot_general x8, matrix products, one_block(): jnp.einsum('cobdr,cdprqa->cobpqa', weight_part, volt_part, preferred_elem...  58 us
    reshape x1, local copies, waits for them, and re-layouts, body(): outgoing = voltages.reshape(inputs_here, 2, time_bins, AVG, chan_count).t...  40.3 us
    transpose x1, local copies, waits for them, and re-layouts, body(): volt_grid.transpose(2, 1, 3, 4, 0, 5)  35.2 us
    transpose x1, local copies, waits for them, and re-layouts, body(): outgoing = voltages.reshape(inputs_here, 2, time_bins, AVG, chan_count).t...  27.9 us
  transfers between devices with their start and end apart: 15, of which 0 were waited for; matrix products, arithmetic and copies ran while one was open for 65% of the time, Pallas kernels for 0%

profile of v1, /device:TPU:0, one launch (start us, length us, event | category | flops | bytes accessed | tf_op | source)
XLA Modules:
  0.0 1001.7 jit_solution(16417237607577709271)
XLA Ops:
  9.1 16.1 %add_bitcast_fusion = f32[8,16,64,128,1]{3,0,2,1,4:T(8,128)S(1)} fusion(bf16[8,31,8192]{2,0,1:T(8,128)(2,1)} %param.5, f32[8192]{0:T(1024)S(1)} %get-tuple-element.69, f32[8192]{0:T(1024)S(1)} %get-tuple-element.70, f32[8192]{0:T(1024)S(1)} %get-tuple-element.71, f32[8192]{0:T(1024)S(1)} %get-tuple-element.72, f32[8192]{0:T(1024)S(1)} %get-tuple-element.73, ...), kind=kLoop, calls=%fused_computation.26 | loop fusion | flops 49283072 | bytes 38273024 | tf_op jit(solution)/shard_map/reshape | solution.py:65
  25.2 7.2 fusion.18
  34.5 27.8 %fusion.12 = f32[8,2,2,16,64,64]{5,4,3,1,0,2:T(8,128)} fusion(f32[1,128,64]{1,2,0:T(8,128)S(1)} %get-tuple-element.92, f32[1,128,64]{1,2,0:T(8,128)S(1)} %get-tuple-element.93, f32[8,1,16,64,128]{4,3,1,2,0:T(8,128)S(1)} %get-tuple-element.51, f32[8,1,16,64,128]{4,3,1,2,0:T(8,128)S(1)} %get-tuple-element.50), kind=kOutput, calls=%fused_computation.18 | convolution fusion | flops 3223339008 | bytes 16842752 | tf_op jit(solution)/shard_map/irskm,qmj->irqsjk/dot_general | solution.py:73
  62.3 12.1 %slice_subtract_fusion = (f32[8,1,1,16,64,64]{5,4,3,1,0,2:T(8,128)}, f32[8,1,1,16,64,64]{5,4,3,1,0,2:T(8,128)}) fusion(f32[8,2,2,16,64,64]{5,4,3,1,0,2:T(8,128)} %fusion.12), kind=kLoop, calls=%fused_computation.21 | loop fusion | flops 1048576 | bytes 12582912 | tf_op jit(solution)/shard_map/sub | solution.py:74
  84.9 27.9 %copy.27 = bf16[1,4096,8,2,16]{4,3,2,1,0:T(2,128)(2,1)} copy(bf16[1,4096,8,2,16]{1,4,3,2,0:T(8,128)(2,1)S(1)} %maximum_bitcast_fusion) | data formatting | bytes 4194304 | tf_op jit(solution)/shard_map/transpose | solution.py:88
  112.8 40.3 %reshape.380 = bf16[1,16,65536]{2,1,0:T(8,128)(2,1)S(1)} reshape(bf16[1,4096,8,2,16]{4,3,2,1,0:T(2,128)(2,1)} %copy.27) | data formatting | bytes 4194304 | tf_op jit(solution)/shard_map/reshape | solution.py:89
  153.2 6.1 constant_dynamic-slice_fusion
  164.3 251.4 %multiply_convert_fusion = (bf16[8,32,1,1024,64,1]{3,4,5,2,1,0:T(8,128)(2,1)}, bf16[8,32,1,1024,64,1]{3,4,5,2,1,0:T(8,128)(2,1)}) fusion(f32[1024,64]{0,1:T(8,128)S(1)} %copy-done, f32[8,32]{1,0:T(8,128)S(1)} %add_convert_fusion), kind=kLoop, calls=%fused_computation.11 | loop fusion | flops 117440512 | bytes 67372032 | tf_op jit(solution)/shard_map/convert_element_type | solution.py:96
  425.0 229.1 %fusion.15 = bf16[8,32,1,1024,64,1]{3,4,5,2,1,0:T(8,128)(2,1)} fusion(f32[1024,64]{0,1:T(8,128)S(1)} %copy-done, f32[8,32]{1,0:T(8,128)S(1)} %add_convert_fusion), kind=kLoop, calls=%fused_computation.19 | loop fusion | flops 134217728 | bytes 33817600 | tf_op jit(solution)/shard_map/neg | solution.py:98
  663.0 86.9 %maximum_maximum_fusion = bf16[8,32,2,1024,64,2]{3,4,5,2,1,0:T(8,128)(2,1)} fusion(bf16[8,32,1,1024,64,1]{3,4,5,2,1,0:T(8,128)(2,1)} %get-tuple-element.85, bf16[8,32,1,1024,64,1]{3,4,5,2,1,0:T(8,128)(2,1)} %get-tuple-element.84, bf16[8,32,1,1024,64,1]{3,4,5,2,1,0:T(8,128)(2,1)} %fusion.15), kind=kLoop, calls=%fused_computation.10 | loop fusion | flops 201326592 | bytes 234881024 | tf_op jit(solution)/shard_map/stack | solution.py:97
  759.0 5.8 dynamic_update_slice.54
  764.8 5.8 dynamic_update_slice.55
  770.6 5.8 dynamic_update_slice.56
  776.4 5.8 dynamic_update_slice.57
  782.2 5.8 dynamic_update_slice.58
  788.0 5.8 dynamic_update_slice.59
  808.5 6.0 dynamic_update_slice.63
  831.9 5.8 dynamic_update_slice.67
  837.7 20.0 %reshape.381 = bf16[1,16,256,8,2,16]{5,4,3,2,1,0:T(2,128)(2,1)} reshape(bf16[1,16,65536]{2,1,0:T(8,128)(2,1)S(1)} %dynamic_update_slice.67) | data formatting | bytes 4194304 | tf_op jit(solution)/shard_map/reshape | solution.py:117
  857.8 35.2 %copy.28 = bf16[256,16,8,2,1,16]{0,5,3,2,1,4:T(8,128)(2,1)S(1)} copy(bf16[256,16,8,2,1,16]{5,3,2,0,1,4:T(2,128)(2,1)} %bitcast.88) | data formatting | bytes 4194304 | tf_op jit(solution)/shard_map/transpose | solution.py:118
  893.0 6.3 reshape.382
  899.2 13.3 %copy.29 = bf16[8,32,64,2,2,1,16]{2,6,4,3,1,5,0:T(8,128)(2,1)} copy(bf16[8,32,64,2,2,1,16]{1,0,6,4,3,2,5:T(8,128)(2,1)} %reshape.382) | data formatting | bytes 4194304 | tf_op jit(solution)/shard_map/while | solution.py:129
  912.6 59.1 %while.10 = (s32[]{:T(128)}, bf16[8,32,1024,1]{2,3,1,0:T(2,128)(2,1)S(1)}, bf16[8,32,2,1024,64,2]{3,4,5,2,1,0:T(8,128)(2,1)}, bf16[8,32,64,2,2,1,16]{2,6,4,3,1,5,0:T(8,128)(2,1)}, s32[]{:T(128)}) while((s32[]{:T(128)}, bf16[8,32,1024,1]{2,3,1,0:T(2,128)(2,1)S(1)}, bf16[8,32,2,1024,64,2]{3,4,5,2,1,0:T(8,128)(2,1)}, ...), condition=%wide.region_3.4_spmd, body=%wide.region_1.3_spmd.sunk | while | flops 541097984 | bytes 17826888 | solution.py:129
  912.6 7.2 fusion.68
  920.0 7.3 fusion.68
  927.4 7.3 fusion.68
  934.7 7.3 fusion.68
  942.1 7.2 fusion.68
  949.5 7.2 fusion.68
  956.9 7.3 fusion.68
  964.3 7.3 fusion.68
  977.3 19.4 %all_to_all.5 = bf16[16,2,8192]{2,1,0:T(2,128)(2,1)S(1)} all-to-all(bf16[16,2,8192]{2,1,0:T(2,128)(2,1)S(1)} %reshape.395), channel_id=1, replica_groups=mesh['grp'=2,'chan'=16] {'chan'}, dimensions={0} | all-to-all | bytes 1048576 | tf_op jit(solution)/shard_map/all_to_all | solution.py:132
  (121 shorter events, 95.8 us)
Async XLA Ops:
  159.3 256.4 %collective-permute-start = (bf16[1,1,65536]{2,1,0:T(2,128)(2,1)}, bf16[1,1,65536]{2,1,0:T(2,128)(2,1)S(1)}, u32[]{:S(2)}, u32[]{:S(2)}) collective-permute-start(bf16[1,1,65536]{2,1,0:T(2,128)(2,1)} %get-tuple-element.66), channel_id=1, source_target_pairs={{0,1},{1,0},{2,3},{3,2},{4,5},{5,4},{6,7},{7,6},{8,9},{9,8},{10,11... | collective-permute-start | bytes 393224 | tf_op jit(solution)/shard_map/ppermute | solution.py:113
  159.8 258.5 %collective-permute-start.1 = (bf16[1,1,65536]{2,1,0:T(2,128)(2,1)}, bf16[1,1,65536]{2,1,0:T(2,128)(2,1)S(1)}, u32[]{:S(2)}, u32[]{:S(2)}) collective-permute-start(bf16[1,1,65536]{2,1,0:T(2,128)(2,1)} %get-tuple-element.65), channel_id=1, source_target_pairs={{0,2},{1,3},{2,0},{3,1},{4,6},{5,7},{6,4},{7,5},{8,10},{9,11},{10,... | collective-permute-start | bytes 393224 | tf_op jit(solution)/shard_map/ppermute | solution.py:113
  162.4 256.2 %collective-permute-start.2 = (bf16[1,1,65536]{2,1,0:T(2,128)(2,1)}, bf16[1,1,65536]{2,1,0:T(2,128)(2,1)S(1)}, u32[]{:S(2)}, u32[]{:S(2)}) collective-permute-start(bf16[1,1,65536]{2,1,0:T(2,128)(2,1)} %get-tuple-element.64), channel_id=1, source_target_pairs={{0,3},{1,2},{2,1},{3,0},{4,7},{5,6},{6,5},{7,4},{8,11},{9,10},{10,... | collective-permute-start | bytes 393224 | tf_op jit(solution)/shard_map/ppermute | solution.py:113
  162.4 258.9 %collective-permute-start.3 = (bf16[1,1,65536]{2,1,0:T(2,128)(2,1)}, bf16[1,1,65536]{2,1,0:T(2,128)(2,1)S(1)}, u32[]{:S(2)}, u32[]{:S(2)}) collective-permute-start(bf16[1,1,65536]{2,1,0:T(2,128)(2,1)} %get-tuple-element.63), channel_id=1, source_target_pairs={{0,4},{1,5},{2,6},{3,7},{4,0},{5,1},{6,2},{7,3},{8,12},{9,13},{10,... | collective-permute-start | bytes 393224 | tf_op jit(solution)/shard_map/ppermute | solution.py:113
  164.2 257.2 %collective-permute-start.4 = (bf16[1,1,65536]{2,1,0:T(2,128)(2,1)}, bf16[1,1,65536]{2,1,0:T(2,128)(2,1)S(1)}, u32[]{:S(2)}, u32[]{:S(2)}) collective-permute-start(bf16[1,1,65536]{2,1,0:T(2,128)(2,1)} %get-tuple-element.62), channel_id=1, source_target_pairs={{0,5},{1,4},{2,7},{3,6},{4,1},{5,0},{6,3},{7,2},{8,13},{9,12},{10,... | collective-permute-start | bytes 393224 | tf_op jit(solution)/shard_map/ppermute | solution.py:113
  164.2 251.5 %copy-start.6 = (bf16[1,1,65536]{2,1,0:T(2,128)(2,1)S(1)}, bf16[1,1,65536]{2,1,0:T(2,128)(2,1)}, u32[]{:S(2)}) copy-start(bf16[1,1,65536]{2,1,0:T(2,128)(2,1)} %get-tuple-element.61) | copy-start | bytes 393220
  164.2 254.2 %copy-start.5 = (bf16[1,1,65536]{2,1,0:T(2,128)(2,1)S(1)}, bf16[1,1,65536]{2,1,0:T(2,128)(2,1)}, u32[]{:S(2)}) copy-start(bf16[1,1,65536]{2,1,0:T(2,128)(2,1)} %get-tuple-element.60) | copy-start | bytes 393220
  164.2 254.3 %copy-start.4 = (bf16[1,1,65536]{2,1,0:T(2,128)(2,1)S(1)}, bf16[1,1,65536]{2,1,0:T(2,128)(2,1)}, u32[]{:S(2)}) copy-start(bf16[1,1,65536]{2,1,0:T(2,128)(2,1)} %get-tuple-element.59) | copy-start | bytes 393220
  164.2 257.1 %copy-start.3 = (bf16[1,1,65536]{2,1,0:T(2,128)(2,1)S(1)}, bf16[1,1,65536]{2,1,0:T(2,128)(2,1)}, u32[]{:S(2)}) copy-start(bf16[1,1,65536]{2,1,0:T(2,128)(2,1)} %get-tuple-element.58) | copy-start | bytes 393220
  164.2 257.1 %copy-start.2 = (bf16[1,1,65536]{2,1,0:T(2,128)(2,1)S(1)}, bf16[1,1,65536]{2,1,0:T(2,128)(2,1)}, u32[]{:S(2)}) copy-start(bf16[1,1,65536]{2,1,0:T(2,128)(2,1)} %get-tuple-element.57) | copy-start | bytes 393220
  415.7 238.4 %copy-start.7 = (bf16[1,1,65536]{2,1,0:T(2,128)(2,1)}, bf16[1,1,65536]{2,1,0:T(2,128)(2,1)S(1)}, u32[]{:S(2)}) copy-start(bf16[1,1,65536]{2,1,0:T(2,128)(2,1)S(1)} %collective-permute-done) | copy-start | bytes 393220
  415.7 238.4 %collective-permute-start.5 = (bf16[1,1,65536]{2,1,0:T(2,128)(2,1)S(1)}, bf16[1,1,65536]{2,1,0:T(2,128)(2,1)S(1)}, u32[]{:S(2)}, u32[]{:S(2)}) collective-permute-start(bf16[1,1,65536]{2,1,0:T(2,128)(2,1)S(1)} %copy-done.6), channel_id=1, source_target_pairs={{0,6},{1,7},{2,4},{3,5},{4,2},{5,3},{6,0},{7,1},{8,14},{9,15},{10,... | collective-permute-start | bytes 393224 | tf_op jit(solution)/shard_map/ppermute | solution.py:113
  418.4 235.7 %copy-start.9 = (bf16[1,1,65536]{2,1,0:T(2,128)(2,1)}, bf16[1,1,65536]{2,1,0:T(2,128)(2,1)S(1)}, u32[]{:S(2)}) copy-start(bf16[1,1,65536]{2,1,0:T(2,128)(2,1)S(1)} %collective-permute-done.1) | copy-start | bytes 393220
  418.4 235.9 %collective-permute-start.6 = (bf16[1,1,65536]{2,1,0:T(2,128)(2,1)S(1)}, bf16[1,1,65536]{2,1,0:T(2,128)(2,1)S(1)}, u32[]{:S(2)}, u32[]{:S(2)}) collective-permute-start(bf16[1,1,65536]{2,1,0:T(2,128)(2,1)S(1)} %copy-done.5), channel_id=1, source_target_pairs={{0,7},{1,6},{2,5},{3,4},{4,3},{5,2},{6,1},{7,0},{8,15},{9,14},{10,... | collective-permute-start | bytes 393224 | tf_op jit(solution)/shard_map/ppermute | solution.py:113
  418.5 235.5 %copy-start.10 = (bf16[1,1,65536]{2,1,0:T(2,128)(2,1)}, bf16[1,1,65536]{2,1,0:T(2,128)(2,1)S(1)}, u32[]{:S(2)}) copy-start(bf16[1,1,65536]{2,1,0:T(2,128)(2,1)S(1)} %collective-permute-done.2) | copy-start | bytes 393220
  418.5 239.4 %collective-permute-start.7 = (bf16[1,1,65536]{2,1,0:T(2,128)(2,1)S(1)}, bf16[1,1,65536]{2,1,0:T(2,128)(2,1)S(1)}, u32[]{:S(2)}, u32[]{:S(2)}) collective-permute-start(bf16[1,1,65536]{2,1,0:T(2,128)(2,1)S(1)} %copy-done.4), channel_id=1, source_target_pairs={{0,8},{1,9},{2,10},{3,11},{4,12},{5,13},{6,14},{7,15},{8,0},{9,1},... | collective-permute-start | bytes 393224 | tf_op jit(solution)/shard_map/ppermute | solution.py:113
  421.3 232.8 %copy-start.11 = (bf16[1,1,65536]{2,1,0:T(2,128)(2,1)}, bf16[1,1,65536]{2,1,0:T(2,128)(2,1)S(1)}, u32[]{:S(2)}) copy-start(bf16[1,1,65536]{2,1,0:T(2,128)(2,1)S(1)} %collective-permute-done.3) | copy-start | bytes 393220
  421.3 236.7 %collective-permute-start.8 = (bf16[1,1,65536]{2,1,0:T(2,128)(2,1)S(1)}, bf16[1,1,65536]{2,1,0:T(2,128)(2,1)S(1)}, u32[]{:S(2)}, u32[]{:S(2)}) collective-permute-start(bf16[1,1,65536]{2,1,0:T(2,128)(2,1)S(1)} %copy-done.3), channel_id=1, source_target_pairs={{0,9},{1,8},{2,11},{3,10},{4,13},{5,12},{6,15},{7,14},{8,1},{9,0},... | collective-permute-start | bytes 393224 | tf_op jit(solution)/shard_map/ppermute | solution.py:113
  421.4 232.7 %copy-start.12 = (bf16[1,1,65536]{2,1,0:T(2,128)(2,1)}, bf16[1,1,65536]{2,1,0:T(2,128)(2,1)S(1)}, u32[]{:S(2)}) copy-start(bf16[1,1,65536]{2,1,0:T(2,128)(2,1)S(1)} %collective-permute-done.4) | copy-start | bytes 393220
  421.4 240.9 %collective-permute-start.9 = (bf16[1,1,65536]{2,1,0:T(2,128)(2,1)S(1)}, bf16[1,1,65536]{2,1,0:T(2,128)(2,1)S(1)}, u32[]{:S(2)}, u32[]{:S(2)}) collective-permute-start(bf16[1,1,65536]{2,1,0:T(2,128)(2,1)S(1)} %copy-done.2), channel_id=1, source_target_pairs={{0,10},{1,11},{2,8},{3,9},{4,14},{5,15},{6,12},{7,13},{8,2},{9,3},... | collective-permute-start | bytes 393224 | tf_op jit(solution)/shard_map/ppermute | solution.py:113
  654.1 95.8 %copy-start.13 = (bf16[1,1,65536]{2,1,0:T(2,128)(2,1)}, bf16[1,1,65536]{2,1,0:T(2,128)(2,1)S(1)}, u32[]{:S(2)}) copy-start(bf16[1,1,65536]{2,1,0:T(2,128)(2,1)S(1)} %collective-permute-done.5) | copy-start | bytes 393220
  654.1 154.4 %collective-permute-start.10 = (bf16[1,1,65536]{2,1,0:T(2,128)(2,1)}, bf16[1,1,65536]{2,1,0:T(2,128)(2,1)}, u32[]{:S(2)}, u32[]{:S(2)}) collective-permute-start(bf16[1,1,65536]{2,1,0:T(2,128)(2,1)} %get-tuple-element.56), channel_id=1, source_target_pairs={{0,11},{1,10},{2,9},{3,8},{4,15},{5,14},{6,13},{7,12},{8,3},{9,2},... | collective-permute-start | bytes 393224 | tf_op jit(solution)/shard_map/ppermute | solution.py:113
  654.3 95.6 %copy-start.14 = (bf16[1,1,65536]{2,1,0:T(2,128)(2,1)}, bf16[1,1,65536]{2,1,0:T(2,128)(2,1)S(1)}, u32[]{:S(2)}) copy-start(bf16[1,1,65536]{2,1,0:T(2,128)(2,1)S(1)} %collective-permute-done.6) | copy-start | bytes 393220
  654.3 160.2 %collective-permute-start.11 = (bf16[1,1,65536]{2,1,0:T(2,128)(2,1)}, bf16[1,1,65536]{2,1,0:T(2,128)(2,1)}, u32[]{:S(2)}, u32[]{:S(2)}) collective-permute-start(bf16[1,1,65536]{2,1,0:T(2,128)(2,1)} %get-tuple-element.55), channel_id=1, source_target_pairs={{0,12},{1,13},{2,14},{3,15},{4,8},{5,9},{6,10},{7,11},{8,4},{9,5},... | collective-permute-start | bytes 393224 | tf_op jit(solution)/shard_map/ppermute | solution.py:113
  657.9 92.0 %copy-start.15 = (bf16[1,1,65536]{2,1,0:T(2,128)(2,1)}, bf16[1,1,65536]{2,1,0:T(2,128)(2,1)S(1)}, u32[]{:S(2)}) copy-start(bf16[1,1,65536]{2,1,0:T(2,128)(2,1)S(1)} %collective-permute-done.7) | copy-start | bytes 393220
  657.9 162.4 %collective-permute-start.12 = (bf16[1,1,65536]{2,1,0:T(2,128)(2,1)S(1)}, bf16[1,1,65536]{2,1,0:T(2,128)(2,1)}, u32[]{:S(2)}, u32[]{:S(2)}) collective-permute-start(bf16[1,1,65536]{2,1,0:T(2,128)(2,1)S(1)} %get-tuple-element.54), channel_id=1, source_target_pairs={{0,13},{1,12},{2,15},{3,14},{4,9},{5,8},{6,11},{7,10},{8,5},{9,4},... | collective-permute-start | bytes 393224 | tf_op jit(solution)/shard_map/ppermute | solution.py:113
  658.0 168.1 %collective-permute-start.13 = (bf16[1,1,65536]{2,1,0:T(2,128)(2,1)S(1)}, bf16[1,1,65536]{2,1,0:T(2,128)(2,1)}, u32[]{:S(2)}, u32[]{:S(2)}) collective-permute-start(bf16[1,1,65536]{2,1,0:T(2,128)(2,1)S(1)} %get-tuple-element.53), channel_id=1, source_target_pairs={{0,14},{1,15},{2,12},{3,13},{4,10},{5,11},{6,8},{7,9},{8,6},{9,7},... | collective-permute-start | bytes 393224 | tf_op jit(solution)/shard_map/ppermute | solution.py:113
  662.3 169.6 %collective-permute-start.14 = (bf16[1,1,65536]{2,1,0:T(2,128)(2,1)S(1)}, bf16[1,1,65536]{2,1,0:T(2,128)(2,1)}, u32[]{:S(2)}, u32[]{:S(2)}) collective-permute-start(bf16[1,1,65536]{2,1,0:T(2,128)(2,1)S(1)} %get-tuple-element.52), channel_id=1, source_target_pairs={{0,15},{1,14},{2,13},{3,12},{4,11},{5,10},{6,9},{7,8},{8,7},{9,6},... | collective-permute-start | bytes 393224 | tf_op jit(solution)/shard_map/ppermute | solution.py:113
  663.0 91.5 %copy-start.8 = (bf16[1,1,65536]{2,1,0:T(2,128)(2,1)S(1)}, bf16[1,1,65536]{2,1,0:T(2,128)(2,1)}, u32[]{:S(2)}) copy-start(bf16[1,1,65536]{2,1,0:T(2,128)(2,1)} %copy-done.7) | copy-start | bytes 393220
  754.5 45.0 %copy-start.17 = (bf16[1,1,65536]{2,1,0:T(2,128)(2,1)S(1)}, bf16[1,1,65536]{2,1,0:T(2,128)(2,1)}, u32[]{:S(2)}) copy-start(bf16[1,1,65536]{2,1,0:T(2,128)(2,1)} %copy-done.16) | copy-start | bytes 393220
  759.0 45.0 %copy-start.19 = (bf16[1,1,65536]{2,1,0:T(2,128)(2,1)S(1)}, bf16[1,1,65536]{2,1,0:T(2,128)(2,1)}, u32[]{:S(2)}) copy-start(bf16[1,1,65536]{2,1,0:T(2,128)(2,1)} %copy-done.18) | copy-start | bytes 393220
  899.2 13.4 %copy-start.1 = (bf16[8,32,1024,1]{2,3,1,0:T(2,128)(2,1)S(1)}, bf16[8,32,1024,1]{2,3,1,0:T(2,128)(2,1)}, u32[]{:S(2)}) copy-start(bf16[8,32,1024,1]{2,3,1,0:T(2,128)(2,1)} %custom-call) | copy-start | bytes 1572868
  (4 other events, 21.0 us)
